TPU v7x, 128 devices: a whole 4x4x4 slice. The times are simulated.
128 devices in a mesh: blk: 16 (over x, y_hi, core), req: 8 (over y_lo, z).
Axes of the slice: x: 4, y: 4 (y_hi: 2, y_lo: 2; y = y_hi * 2 + y_lo), z: 4, core: 2. Of those that a mesh axis runs over, the one named last changes fastest.
Arguments:
- long_q: bfloat16 [16384, 2048], P('blk', 'req'), may hold values from -6 to 6
- long_k: bfloat16 [16384, 2048], P('blk', 'req'), may hold values from -6 to 6
- long_v: bfloat16 [16384, 2048], P('blk', 'req'), may hold values from -6 to 6
- short_q: bfloat16 [8192, 2048], P('blk', 'req'), may hold values from -6 to 6
- short_k: bfloat16 [8192, 2048], P('blk', 'req'), may hold values from -6 to 6
- short_v: bfloat16 [8192, 2048], P('blk', 'req'), may hold values from -6 to 6
- short_seg: int32 [16, 512], P('blk'), may hold values from 0 to 15, never falling along the last dimension, each value on 1 to 96 neighbouring positions
- pool_kv: bfloat16 [1024, 2, 16, 2048], P('blk', None, None, 'req'), may hold values from -6 to 6
- page_table: int32 [16, 16, 4], replicated, may hold values from 0 to 1023, as said below
- w_out: bfloat16 [2048, 2048], replicated, may hold values from -0.125 to 0.125
Outputs:
- long_out: bfloat16 [16384, 2048], P(('blk', 'req'))
- short_out: bfloat16 [8192, 2048], P(('blk', 'req'))
Inputs may be any that keep to these rules, and one draw needn't show every extreme that they name: `short_seg`: along each pack the request numbers never fall, and each of the 16 requests has 1 to 96 tokens, one of them exactly 96. `page_table`: entry [b, s, j] is o * 64 + i for page i of the pool rows held by index o of blk; for every pack b and every o exactly 4 of the 64 entries of b name pages of o.
All inputs are finite; a program needn't handle non-finite values.
Results may differ from a plain program's by a relative error of at most 0.015.
Values may be sent and summed in bfloat16 or wider, within the bound.
No kernel may reach another device: no remote copies, remote signals or barrier semaphores. Data moves between devices by JAX's collectives and lax.ppermute only.
A program may use at most 128 MiB of HBM per device.

v0:
```python
import math
import jax
import jax.numpy as jnp
from jax import lax
from jax.sharding import PartitionSpec as P

HD = 128
PPS = 4
very_negative = -1e30


def fold_block(state_now, query_heads, query_pos, key_block, value_block, block_first):
    acc_sum, run_max, run_total = state_now
    heads_dev = query_heads.shape[1]
    key_heads = key_block.reshape(key_block.shape[0], heads_dev, HD)
    value_heads = value_block.reshape(value_block.shape[0], heads_dev, HD)
    scores = jnp.einsum(
        "qhd,khd->hqk", query_heads, key_heads, preferred_element_type=jnp.float32
    ) * HD ** (-0.5)
    key_pos = block_first + jnp.arange(key_block.shape[0], dtype=jnp.int32)
    allowed = (key_pos[None, :] <= query_pos[:, None])[None]
    scores = jnp.where(allowed, scores, very_negative)
    new_max = jnp.maximum(run_max, jnp.max(scores, axis=-1))
    weights = jnp.where(allowed, jnp.exp(scores - new_max[..., None]), 0.0)
    factor = jnp.exp(run_max - new_max)
    run_total = run_total * factor + jnp.sum(weights, axis=-1)
    acc_sum = acc_sum * factor[..., None] + jnp.einsum(
        "hqk,khd->hqd",
        weights.astype(jnp.bfloat16),
        value_heads,
        preferred_element_type=jnp.float32,
    )
    return (acc_sum, new_max, run_total)


def prompt_attention(queries, query_pos, long_k, long_v):
    row_count, width = queries.shape
    heads_dev = width // HD
    query_heads = queries.reshape(row_count, heads_dev, HD)
    last_pos = jnp.max(query_pos)
    init = (
        jnp.zeros((heads_dev, row_count, HD), jnp.float32),
        jnp.full((heads_dev, row_count), very_negative, jnp.float32),
        jnp.zeros((heads_dev, row_count), jnp.float32),
    )
    key_piece = lax.all_gather(long_k, "blk", axis=0, tiled=True)
    value_piece = lax.all_gather(long_v, "blk", axis=0, tiled=True)
    piece_rows = key_piece.shape[0]
    step_rows = math.gcd(piece_rows, 1024)

    def one_step(block_num, state_in):
        block_start = block_num * step_rows
        key_block = lax.dynamic_slice_in_dim(key_piece, block_start, step_rows, 0)
        value_block = lax.dynamic_slice_in_dim(value_piece, block_start, step_rows, 0)

        def compute_block(state_live):
            return fold_block(
                state_live, query_heads, query_pos, key_block, value_block, block_start
            )

        def keep_state(state_skip):
            return state_skip

        return lax.cond(block_start <= last_pos, compute_block, keep_state, state_in)

    acc_sum, run_max, run_total = lax.fori_loop(0, piece_rows // step_rows, one_step, init)
    merged = acc_sum / run_total[..., None]
    return merged.transpose(1, 0, 2).reshape(row_count, width).astype(jnp.bfloat16)


def pack_attention(
    short_q, short_k, short_v, short_seg, pool_kv, page_table, block_index, block_count
):
    pack_rows, width = short_q.shape
    heads_dev = width // HD
    pool_pages = pool_kv.shape[0]
    page_len = pool_kv.shape[2]
    page_rows = page_table.reshape(block_count, -1)
    entries = page_rows.shape[1]
    capacity = entries // block_count
    owners = page_rows // pool_pages
    places = page_rows % pool_pages
    wanted = owners == block_index
    ranks = jnp.cumsum(wanted.astype(jnp.int32), axis=1) - 1
    picked = wanted[:, :, None] & (
        ranks[:, :, None] == jnp.arange(capacity, dtype=jnp.int32)[None, None, :]
    )
    send_places = jnp.sum(jnp.where(picked, places[:, :, None], 0), axis=1)
    outgoing = pool_kv[send_places.reshape(-1)].reshape(block_count, capacity, 2, page_len, width)
    arrived = lax.all_to_all(outgoing, "blk", split_axis=0, concat_axis=0, tiled=True)
    my_owners = lax.dynamic_index_in_dim(owners, block_index, 0, keepdims=False)
    order = jnp.arange(entries, dtype=jnp.int32)
    before = (my_owners[None, :] == my_owners[:, None]) & (order[None, :] < order[:, None])
    slots = my_owners * capacity + jnp.sum(before.astype(jnp.int32), axis=1)
    fetched = arrived.reshape(block_count * capacity, 2, page_len, width)[slots]
    cache_len = entries * page_len
    key_rows = jnp.concatenate([fetched[:, 0].reshape(cache_len, width), short_k], 0)
    value_rows = jnp.concatenate([fetched[:, 1].reshape(cache_len, width), short_v], 0)
    segment = short_seg[0]
    positions = jnp.arange(pack_rows, dtype=jnp.int32)
    key_seg = jnp.concatenate([jnp.arange(cache_len, dtype=jnp.int32) // (PPS * page_len), segment])
    key_pos = jnp.concatenate([jnp.full((cache_len,), -1, jnp.int32), positions])
    allowed = ((key_seg[None, :] == segment[:, None]) & (key_pos[None, :] <= positions[:, None]))[
        None
    ]
    query_heads = short_q.reshape(pack_rows, heads_dev, HD)
    key_heads = key_rows.reshape(cache_len + pack_rows, heads_dev, HD)
    value_heads = value_rows.reshape(cache_len + pack_rows, heads_dev, HD)
    scores = jnp.einsum(
        "qhd,khd->hqk", query_heads, key_heads, preferred_element_type=jnp.float32
    ) * HD ** (-0.5)
    scores = jnp.where(allowed, scores, very_negative)
    row_max = jnp.max(scores, axis=-1)
    weights = jnp.where(allowed, jnp.exp(scores - row_max[..., None]), 0.0)
    total = jnp.sum(weights, axis=-1)
    numer = jnp.einsum(
        "hqk,khd->hqd",
        weights.astype(jnp.bfloat16),
        value_heads,
        preferred_element_type=jnp.float32,
    )
    merged = numer / total[..., None]
    return merged.transpose(1, 0, 2).reshape(pack_rows, width).astype(jnp.bfloat16)


def per_device(
    long_q, long_k, long_v, short_q, short_k, short_v, short_seg, pool_kv, page_table, w_out
):
    block_count = lax.axis_size("blk")
    block_index = lax.axis_index("blk")
    group_index = lax.axis_index("req")
    row_count, width = long_q.shape
    query_pos = block_index * row_count + jnp.arange(row_count, dtype=jnp.int32)
    long_attn = prompt_attention(long_q, query_pos, long_k, long_v)
    short_attn = pack_attention(
        short_q, short_k, short_v, short_seg, pool_kv, page_table, block_index, block_count
    )
    w_rows = lax.dynamic_slice_in_dim(w_out, group_index * width, width, 0)
    long_out = lax.psum_scatter(
        jnp.dot(long_attn, w_rows, preferred_element_type=jnp.float32).astype(jnp.bfloat16),
        "req",
        scatter_dimension=0,
        tiled=True,
    )
    short_out = lax.psum_scatter(
        jnp.dot(short_attn, w_rows, preferred_element_type=jnp.float32).astype(jnp.bfloat16),
        "req",
        scatter_dimension=0,
        tiled=True,
    )
    return (long_out, short_out)


def solution(mesh):
    placed = (
        P("blk", "req"),
        P("blk", "req"),
        P("blk", "req"),
        P("blk", "req"),
        P("blk", "req"),
        P("blk", "req"),
        P("blk", None),
        P("blk", None, None, "req"),
        P(),
        P(),
    )
    return jax.shard_map(
        per_device,
        mesh=mesh,
        in_specs=placed,
        out_specs=(P(("blk", "req"), None), P(("blk", "req"), None)),
        check_vma=False,
    )
```

profile of v0, /device:TPU:1, one launch (start us, length us, event | category | flops | bytes accessed | tf_op | source)
XLA Modules:
  0.0 403.9 jit_solution(17348322285215755611)
XLA Ops:
  8.1 2.1 copy.40
  10.3 2.1 copy.42
  12.4 0.8 copy.45
  13.9 1.6 gather_fusion
  15.5 8.4 %all-to-all-start = ((bf16[16,4,2,16,256]{4,3,2,1,0:T(8,128)(2,1)}), bf16[16,4,2,16,256]{4,3,2,1,0:T(8,128)(2,1)S(1)}, u32[]{:S(2)}, u32[]{:S(2)}) async-start(bf16[16,4,2,16,256]{4,3,2,1,0:T(8,128)(2,1)} %bitcast.9), calls=%async_computation.1 | async-start | bytes 2097152 | tf_op jit(solution)/shard_map/all_to_all | solution.py:90
  24.2 0.8 copy.53
  25.4 1.9 fusion.20
  27.3 17.5 %all-to-all-done = bf16[16,4,2,16,256]{4,3,2,1,0:T(8,128)(2,1)S(1)} async-done(((bf16[16,4,2,16,256]{4,3,2,1,0:T(8,128)(2,1)}), bf16[16,4,2,16,256]{4,3,2,1,0:T(8,128)(2,1)S(1)}, u32[]{:S(2)}, u32[]{:S(2)}) %all-to-all-start) | async-done | bytes 1048608 | tf_op jit(solution)/shard_map/all_to_all | solution.py:90
  44.8 0.6 gather_fusion.1
  45.4 0.9 fusion.64
  46.3 1.2 concatenate.21
  48.1 6.6 %fusion.65 = (f32[2,512]{1,0:T(2,128)S(1)}, bf16[2,512,1536]{1,2,0:T(8,128)(2,1)}) fusion(pred[512,1536]{0,1:T(8,128)(4,1)} %fusion.20, bf16[512,2,128]{2,0,1:T(8,128)(2,1)} %copy.53, bf16[1024,2,128]{2,0,1:T(8,128)(2,1)S(1)} %copy.52, bf16[512,256]{1,0:T(8,128)(2,1)} %param.17), kind=kOutput, calls=%fused_computation.93 | convolution fusion | flops 413664768 | bytes 4984832 | tf_op jit(solution)/shard_map/sub | solution.py:114
  54.7 2.5 fusion.28
  57.2 3.3 convolution_convert_fusion.1
  60.8 0.6 add_reduce_fusion
  61.9 35.7 %all-gather.3.cloned.1.call-done = bf16[16384,256]{0,1:T(8,128)(2,1)} async-done(((bf16[1024,256]{0,1:T(8,128)(2,1)}), bf16[16384,256]{0,1:T(8,128)(2,1)}) %all-gather.3.cloned.1.call-update) | async-done | bytes 8388624 | tf_op jit(solution)/shard_map/all_gather | solution.py:46
  97.6 73.6 %all-gather.5.cloned.1.call-done = bf16[16384,256]{0,1:T(8,128)(2,1)} async-done(((bf16[1024,256]{0,1:T(8,128)(2,1)}), bf16[16384,256]{0,1:T(8,128)(2,1)}) %all-gather.5.cloned.1.call-update) | async-done | bytes 8388624 | tf_op jit(solution)/shard_map/all_gather | solution.py:47
  171.4 30.6 %while.18 = (s32[]{:T(128)}, f32[2,1024,128]{2,1,0:T(8,128)S(1)}, f32[2,1024]{1,0:T(2,128)S(1)}, f32[2,1024]{1,0:T(2,128)S(1)}, s32[]{:T(128)}, /*index=5*/bf16[...) while((s32[]{:T(128)}, f32[2,1024,128]{2,1,0:T(8,128)S(1)}, ...), condition=%wide.region_6.7_spmd.clone, body=%wide.region_1.6_spmd.clone.sunk | while | flops 1102583808 | bytes 35283264 | solution.py:66
  172.0 10.0 %conditional.3 = ((f32[2,1024,128]{2,1,0:T(8,128)S(1)}, f32[2,1024]{1,0:T(2,128)S(1)}, f32[2,1024]{1,0:T(2,128)S(1)})) conditional(s32[]{:T(128)} %convert_element_type.77, (f32[2,1024,128]{2,1,0:T(8,128)S(1)}, f32[2,1024]{1,0:T(2,128)S(1)}, f32[2,1024]{1,0:T(2,128)S(1)}) %tuple.66, (s32[]{:T(128)}, s32[]{:T(128)}, bf16[16384,256]{0,1:T(8,128)(2,1)}, ...), branch_computations={%region_2.0_spmd, %region_3.5_spmd} | conditional | flops 1102583808 | bytes 35278928 | solution.py:64
  172.0 1.3 constant_dynamic-slice_fusion
  173.3 0.7 broadcast_compare_fusion
  174.0 2.0 fusion.2
  176.0 2.3 fusion.3
  178.3 3.7 fusion.8
  182.7 10.0 %conditional.3 = ((f32[2,1024,128]{2,1,0:T(8,128)S(1)}, f32[2,1024]{1,0:T(2,128)S(1)}, f32[2,1024]{1,0:T(2,128)S(1)})) conditional(s32[]{:T(128)} %convert_element_type.77, (f32[2,1024,128]{2,1,0:T(8,128)S(1)}, f32[2,1024]{1,0:T(2,128)S(1)}, f32[2,1024]{1,0:T(2,128)S(1)}) %tuple.66, (s32[]{:T(128)}, s32[]{:T(128)}, bf16[16384,256]{0,1:T(8,128)(2,1)}, ...), branch_computations={%region_2.0_spmd, %region_3.5_spmd} | conditional | flops 1102583808 | bytes 35278928 | solution.py:64
  182.7 1.3 constant_dynamic-slice_fusion
  184.0 0.7 broadcast_compare_fusion
  184.6 2.0 fusion.2
  186.6 2.3 fusion.3
  188.9 3.7 fusion.8
  202.5 4.5 %convolution_convert_fusion = bf16[1024,2048]{1,0:T(8,128)(2,1)} fusion(bf16[1024,256]{0,1:T(8,128)(2,1)S(1)} %bitcast.78, bf16[2048,2048]{1,0:T(8,128)(2,1)} %param.23, s32[]{:T(128)S(6)} %select_n.90), kind=kOutput, calls=%fused_computation.25 | convolution fusion | flops 1075838976 | bytes 5767172 | tf_op jit(solution)/shard_map/dot_general | solution.py:140
  207.0 189.5 %reduce-scatter.3.cloned.1.call-done = bf16[128,2048]{1,0:T(8,128)(2,1)} async-done(((bf16[1024,2048]{1,0:T(8,128)(2,1)}), bf16[128,2048]{1,0:T(8,128)(2,1)}) %reduce-scatter.3.cloned.1.call-update) | async-done | bytes 524304 | tf_op jit(solution)/shard_map/reduce_scatter | solution.py:139
  (87 shorter events, 3.6 us)
Async XLA Ops:
  8.0 5.9 %copy-start = (bf16[64,2,16,256]{3,2,1,0:T(8,128)(2,1)S(1)}, bf16[64,2,16,256]{3,2,1,0:T(8,128)(2,1)}, u32[]{:S(2)}) copy-start(bf16[64,2,16,256]{3,2,1,0:T(8,128)(2,1)} %param.21) | copy-start | bytes 3145732
  8.0 17.4 %copy-start.4 = (s32[1536]{0:T(1024)S(1)}, s32[1536]{0:T(1024)}, u32[]{:S(2)}) copy-start(s32[1536]{0:T(1024)} %constant.138.clone.1) | copy-start | bytes 18436
  8.0 16.0 %copy-start.2 = (bf16[512,256]{1,0:T(8,128)(2,1)S(1)}, bf16[512,256]{1,0:T(8,128)(2,1)}, u32[]{:S(2)}) copy-start(bf16[512,256]{1,0:T(8,128)(2,1)} %param.18) | copy-start | bytes 786436
  8.0 17.0 %copy-start.3 = (bf16[512,256]{1,0:T(8,128)(2,1)S(1)}, bf16[512,256]{1,0:T(8,128)(2,1)}, u32[]{:S(2)}) copy-start(bf16[512,256]{1,0:T(8,128)(2,1)} %param.19) | copy-start | bytes 786436
  8.0 17.4 %copy-start.5 = (s32[1,512]{1,0:T(1,128)S(1)}, s32[1,512]{1,0:T(1,128)}, u32[]{:S(2)}) copy-start(s32[1,512]{1,0:T(1,128)} %param.20) | copy-start | bytes 6148
  8.1 89.6 %all-gather.3.cloned.1.call-start = ((), (), s32[]{:S(2)}) async-start(), calls=%async_computation.3 | async-start | bytes 8912896 | tf_op jit(solution)/shard_map/all_gather | solution.py:46
  10.3 161.0 %all-gather.5.cloned.1.call-start = ((), (), s32[]{:S(2)}) async-start(), calls=%async_computation.4 | async-start | bytes 8912896 | tf_op jit(solution)/shard_map/all_gather | solution.py:47
  15.5 29.3 %all-to-all-start = ((bf16[16,4,2,16,256]{4,3,2,1,0:T(8,128)(2,1)}), bf16[16,4,2,16,256]{4,3,2,1,0:T(8,128)(2,1)S(1)}, u32[]{:S(2)}, u32[]{:S(2)}) async-start(bf16[16,4,2,16,256]{4,3,2,1,0:T(8,128)(2,1)} %bitcast.9), calls=%async_computation.1 | async-start | bytes 2097152 | tf_op jit(solution)/shard_map/all_to_all | solution.py:90
  24.0 183.0 %reduce-scatter.5.cloned.1.call-start = ((), (), s32[]{:S(2)}) async-start(), calls=%async_computation.6 | async-start | bytes 2359296 | tf_op jit(solution)/shard_map/reduce_scatter | solution.py:145
  54.7 6.8 %copy-start.1 = (bf16[1024,256]{1,0:T(8,128)(2,1)S(1)}, bf16[1024,256]{1,0:T(8,128)(2,1)}, u32[]{:S(2)}) copy-start(bf16[1024,256]{1,0:T(8,128)(2,1)} %param.14) | copy-start | bytes 1572868
  60.6 335.9 %reduce-scatter.3.cloned.1.call-start = ((), (), s32[]{:S(2)}) async-start(), calls=%async_computation.5 | async-start | bytes 4718592 | tf_op jit(solution)/shard_map/reduce_scatter | solution.py:139
Sparse Core Ops, SparseCore 0:
  11.9 85.6 all-gather.2
  100.1 71.1 all-gather.4
Sparse Core Ops, SparseCore 1:
  60.7 49.7 reduce-scatter.4
  207.1 189.4 reduce-scatter.2
where the time goes:
time: 405 us; the launch traced here: 404 us
  waiting for transfers between devices  316 us (78%)
  matrix products  28.3 us (7%)
  between operations  15.8 us (4%)
  local copies, waits for them, and re-layouts  14.8 us (4%)
  loops' own time  10.8 us (3%)
  other arithmetic  9.14 us (2%)
  starting transfers between devices  8.79 us (2%)
    reduce_scatter x1, waiting for transfers between devices, per_device(): lax.psum_scatter(jnp.dot(long_attn, w_rows, preferred_element_type=jnp.fl...  189 us
    all_gather x1, waiting for transfers between devices, prompt_attention(): value_piece = lax.all_gather(long_v, 'blk', axis=0, tiled=True)  73.6 us
    all_gather x1, waiting for transfers between devices, prompt_attention(): key_piece = lax.all_gather(long_k, 'blk', axis=0, tiled=True)  35.7 us
    all_to_all x1, waiting for transfers between devices, pack_attention(): lax.all_to_all(outgoing, 'blk', split_axis=0, concat_axis=0, tiled=True)  17.5 us
    another operation x1, loops' own time, prompt_attention(): lax.fori_loop(0, piece_rows // step_rows, one_step, init)  10.4 us
    all_to_all x1, starting transfers between devices, pack_attention(): lax.all_to_all(outgoing, 'blk', split_axis=0, concat_axis=0, tiled=True)  8.45 us
  transfers between devices with their start and end apart: 5, of which 4 were waited for; matrix products, arithmetic and copies ran while one was open for 12% of the time, Pallas kernels for 0%

commit v1 on v0

--- a/solution.py
+++ b/solution.py
@@ -43,8 +43,11 @@
         jnp.full((heads_dev, row_count), very_negative, jnp.float32),
         jnp.zeros((heads_dev, row_count), jnp.float32),
     )
-    key_piece = lax.all_gather(long_k, "blk", axis=0, tiled=True)
-    value_piece = lax.all_gather(long_v, "blk", axis=0, tiled=True)
+    key_piece, value_piece = jnp.split(
+        lax.all_gather(jnp.concatenate([long_k, long_v], axis=1), "blk", tiled=True, axis=0),
+        [long_k.shape[1]],
+        axis=1,
+    )
     piece_rows = key_piece.shape[0]
     step_rows = math.gcd(piece_rows, 1024)
 

time: 405 us -> 380 us (0.938)
  waiting for transfers between devices: 316 us -> 283 us
  local copies, waits for them, and re-layouts: 14.8 us -> 23.7 us
    all_gather x2 -> x1, waiting for transfers between devices: 109 us -> 74.8 us  [prompt_attention(): lax.all_gather(jnp.concatenate([long_k, long_v], axis=1), 'blk', tiled=Tr...]
    split x0 -> x1, local copies, waits for them, and re-layouts: none -> 11.5 us  [prompt_attention(): jnp.split(lax.all_gather(jnp.concatenate([long_k, long_v], axis=1), 'blk'...]
  transfers between devices with their start and end apart: 5 -> 4, of which waited for: 4 -> 3; matrix products, arithmetic and copies ran while one was open for 12% -> 15% of each run, Pallas kernels for 0% -> 0%
where the time goes in v1:
time: 380 us
  waiting for transfers between devices  283 us (74%)
  matrix products  27.8 us (7%)
  local copies, waits for them, and re-layouts  23.7 us (6%)
  between operations  15.8 us (4%)
  loops' own time  11 us (3%)
  other arithmetic  9.49 us (2%)
  starting transfers between devices  8.75 us (2%)
    reduce_scatter x1, waiting for transfers between devices, per_device(): lax.psum_scatter(jnp.dot(long_attn, w_rows, preferred_element_type=jnp.fl...  190 us
    all_gather x1, waiting for transfers between devices, prompt_attention(): lax.all_gather(jnp.concatenate([long_k, long_v], axis=1), 'blk', tiled=Tr...  74.8 us
    all_to_all x1, waiting for transfers between devices, pack_attention(): lax.all_to_all(outgoing, 'blk', split_axis=0, concat_axis=0, tiled=True)  18.6 us
    split x1, local copies, waits for them, and re-layouts, prompt_attention(): jnp.split(lax.all_gather(jnp.concatenate([long_k, long_v], axis=1), 'blk'...  11.5 us
    another operation x1, loops' own time, prompt_attention(): lax.fori_loop(0, piece_rows // step_rows, one_step, init)  10.7 us
    all_to_all x1, starting transfers between devices, pack_attention(): lax.all_to_all(outgoing, 'blk', split_axis=0, concat_axis=0, tiled=True)  8.45 us
  transfers between devices with their start and end apart: 4, of which 3 were waited for; matrix products, arithmetic and copies ran while one was open for 15% of the time, Pallas kernels for 0%

profile of v1, /device:TPU:1, one launch (start us, length us, event | category | flops | bytes accessed | tf_op | source)
XLA Modules:
  0.0 379.5 jit_solution(1840954491921131011)
XLA Ops:
  8.1 1.4 copy.40
  9.5 1.3 copy.41
  10.8 1.0 pad_maximum_fusion
  11.8 0.8 copy.45
  13.4 1.6 gather_fusion
  15.0 8.4 %all-to-all-start = ((bf16[16,4,2,16,256]{4,3,2,1,0:T(8,128)(2,1)}), bf16[16,4,2,16,256]{4,3,2,1,0:T(8,128)(2,1)S(1)}, u32[]{:S(2)}, u32[]{:S(2)}) async-start(bf16[16,4,2,16,256]{4,3,2,1,0:T(8,128)(2,1)} %bitcast.9), calls=%async_computation.1 | async-start | bytes 2097152 | tf_op jit(solution)/shard_map/all_to_all | solution.py:93
  23.6 0.8 copy.53
  24.5 0.8 copy.55
  25.3 0.7 add_reduce_fusion
  26.7 1.2 fusion.20
  27.9 18.6 %all-to-all-done = bf16[16,4,2,16,256]{4,3,2,1,0:T(8,128)(2,1)S(1)} async-done(((bf16[16,4,2,16,256]{4,3,2,1,0:T(8,128)(2,1)}), bf16[16,4,2,16,256]{4,3,2,1,0:T(8,128)(2,1)S(1)}, u32[]{:S(2)}, u32[]{:S(2)}) %all-to-all-start) | async-done | bytes 1048608 | tf_op jit(solution)/shard_map/all_to_all | solution.py:93
  46.5 0.6 gather_fusion.1
  48.0 6.1 %fusion.66 = (f32[2,512]{1,0:T(2,128)S(1)}, bf16[2,512,1536]{1,2,0:T(8,128)(2,1)}) fusion(pred[512,1536]{0,1:T(8,128)(4,1)S(1)} %fusion.20, bf16[512,2,128]{2,0,1:T(8,128)(2,1)} %copy.53, bf16[1024,2,128]{2,0,1:T(8,128)(2,1)S(1)} %copy.52, bf16[512,256]{1,0:T(8,128)(2,1)} %param.17), kind=kOutput, calls=%fused_computation.95 | convolution fusion | flops 413664768 | bytes 4984832 | tf_op jit(solution)/shard_map/sub | solution.py:117
  54.1 2.5 fusion.28
  56.6 3.3 convolution_convert_fusion.1
  60.1 74.8 %all-gather.2.cloned.1.call-done = bf16[16384,512]{0,1:T(8,128)(2,1)} async-done(((bf16[1024,512]{0,1:T(8,128)(2,1)}), bf16[16384,512]{0,1:T(8,128)(2,1)}) %all-gather.2.cloned.1.call-update) | async-done | bytes 16777232 | tf_op jit(solution)/shard_map/all_gather | solution.py:47
  134.9 11.5 %fusion.64 = (bf16[16384,256]{0,1:T(8,128)(2,1)}, bf16[16384,256]{0,1:T(8,128)(2,1)}) fusion(bf16[16384,512]{0,1:T(8,128)(2,1)} %all-gather.2.cloned.1.call-done), kind=kLoop, calls=%fused_computation.93 | loop fusion | bytes 33554432 | tf_op jit(solution)/shard_map/split | solution.py:46
  146.6 30.9 %while.18 = (s32[]{:T(128)}, f32[2,1024,128]{2,1,0:T(8,128)S(1)}, f32[2,1024]{1,0:T(2,128)S(1)}, f32[2,1024]{1,0:T(2,128)S(1)}, s32[]{:T(128)}, /*index=5*/bf16[...) while((s32[]{:T(128)}, f32[2,1024,128]{2,1,0:T(8,128)S(1)}, ...), condition=%wide.region_6.7_spmd.clone, body=%wide.region_1.6_spmd.clone.sunk | while | flops 1102583808 | bytes 35283256 | solution.py:69
  147.2 10.0 %conditional.3 = ((f32[2,1024,128]{2,1,0:T(8,128)S(1)}, f32[2,1024]{1,0:T(2,128)S(1)}, f32[2,1024]{1,0:T(2,128)S(1)})) conditional(s32[]{:T(128)} %convert_element_type.77, (f32[2,1024,128]{2,1,0:T(8,128)S(1)}, f32[2,1024]{1,0:T(2,128)S(1)}, f32[2,1024]{1,0:T(2,128)S(1)}) %tuple.67, (s32[]{:T(128)}, s32[]{:T(128)}, bf16[16384,256]{0,1:T(8,128)(2,1)}, ...), branch_computations={%region_2.0_spmd, %region_3.5_spmd} | conditional | flops 1102583808 | bytes 35278928 | solution.py:67
  147.3 0.7 broadcast_compare_fusion
  147.9 1.3 constant_dynamic-slice_fusion
  149.2 2.0 fusion.2
  151.2 2.3 fusion.3
  153.5 3.7 fusion.8
  157.9 10.0 %conditional.3 = ((f32[2,1024,128]{2,1,0:T(8,128)S(1)}, f32[2,1024]{1,0:T(2,128)S(1)}, f32[2,1024]{1,0:T(2,128)S(1)})) conditional(s32[]{:T(128)} %convert_element_type.77, (f32[2,1024,128]{2,1,0:T(8,128)S(1)}, f32[2,1024]{1,0:T(2,128)S(1)}, f32[2,1024]{1,0:T(2,128)S(1)}) %tuple.67, (s32[]{:T(128)}, s32[]{:T(128)}, bf16[16384,256]{0,1:T(8,128)(2,1)}, ...), branch_computations={%region_2.0_spmd, %region_3.5_spmd} | conditional | flops 1102583808 | bytes 35278928 | solution.py:67
  157.9 0.7 broadcast_compare_fusion
  158.6 1.3 constant_dynamic-slice_fusion
  159.9 2.0 fusion.2
  161.9 2.3 fusion.3
  164.1 3.7 fusion.8
  177.9 4.5 %convolution_convert_fusion = bf16[1024,2048]{1,0:T(8,128)(2,1)} fusion(bf16[1024,256]{0,1:T(8,128)(2,1)S(1)} %bitcast.78, bf16[2048,2048]{1,0:T(8,128)(2,1)} %param.23, s32[]{:T(128)S(6)} %select_n.90), kind=kOutput, calls=%fused_computation.25 | convolution fusion | flops 1075838976 | bytes 5767172 | tf_op jit(solution)/shard_map/dot_general | solution.py:143
  182.5 189.6 %reduce-scatter.3.cloned.1.call-done = bf16[128,2048]{1,0:T(8,128)(2,1)} async-done(((bf16[1024,2048]{1,0:T(8,128)(2,1)}), bf16[128,2048]{1,0:T(8,128)(2,1)}) %reduce-scatter.3.cloned.1.call-update) | async-done | bytes 524304 | tf_op jit(solution)/shard_map/reduce_scatter | solution.py:142
  (90 shorter events, 3.5 us)
Async XLA Ops:
  8.0 5.4 %copy-start = (bf16[64,2,16,256]{3,2,1,0:T(8,128)(2,1)S(1)}, bf16[64,2,16,256]{3,2,1,0:T(8,128)(2,1)}, u32[]{:S(2)}) copy-start(bf16[64,2,16,256]{3,2,1,0:T(8,128)(2,1)} %param.21) | copy-start | bytes 3145732
  8.0 15.4 %copy-start.3 = (bf16[512,256]{1,0:T(8,128)(2,1)S(1)}, bf16[512,256]{1,0:T(8,128)(2,1)}, u32[]{:S(2)}) copy-start(bf16[512,256]{1,0:T(8,128)(2,1)} %param.18) | copy-start | bytes 786436
  8.0 16.4 %copy-start.4 = (bf16[512,256]{1,0:T(8,128)(2,1)S(1)}, bf16[512,256]{1,0:T(8,128)(2,1)}, u32[]{:S(2)}) copy-start(bf16[512,256]{1,0:T(8,128)(2,1)} %param.19) | copy-start | bytes 786436
  8.0 17.9 %copy-start.2 = (bf16[1024,256]{1,0:T(8,128)(2,1)S(1)}, bf16[1024,256]{1,0:T(8,128)(2,1)}, u32[]{:S(2)}) copy-start(bf16[1024,256]{1,0:T(8,128)(2,1)} %param.14) | copy-start | bytes 1572868
  8.0 126.9 %all-gather.2.cloned.1.call-start = ((), (), s32[]{:S(2)}) async-start(), calls=%async_computation.3 | async-start | bytes 17825792 | tf_op jit(solution)/shard_map/all_gather | solution.py:47
  9.5 17.2 %copy-start.7 = (s32[1,512]{1,0:T(1,128)S(1)}, s32[1,512]{1,0:T(1,128)}, u32[]{:S(2)}) copy-start(s32[1,512]{1,0:T(1,128)} %param.20) | copy-start | bytes 6148
  9.5 17.2 %copy-start.6 = (s32[1536]{0:T(1024)S(1)}, s32[1536]{0:T(1024)}, u32[]{:S(2)}) copy-start(s32[1536]{0:T(1024)} %constant.138.clone.1) | copy-start | bytes 18436
  15.0 31.5 %all-to-all-start = ((bf16[16,4,2,16,256]{4,3,2,1,0:T(8,128)(2,1)}), bf16[16,4,2,16,256]{4,3,2,1,0:T(8,128)(2,1)S(1)}, u32[]{:S(2)}, u32[]{:S(2)}) async-start(bf16[16,4,2,16,256]{4,3,2,1,0:T(8,128)(2,1)} %bitcast.9), calls=%async_computation.1 | async-start | bytes 2097152 | tf_op jit(solution)/shard_map/all_to_all | solution.py:93
  23.4 159.1 %reduce-scatter.5.cloned.1.call-start = ((), (), s32[]{:S(2)}) async-start(), calls=%async_computation.5 | async-start | bytes 2359296 | tf_op jit(solution)/shard_map/reduce_scatter | solution.py:148
  47.9 6.1 %copy-start.5 = (bf16[512,256]{0,1:T(8,128)(2,1)S(1)}, bf16[512,256]{0,1:T(8,128)(2,1)}, u32[]{:S(2)}) copy-start(bf16[512,256]{0,1:T(8,128)(2,1)} %copy.55) | copy-start | bytes 786436
  59.9 312.2 %reduce-scatter.3.cloned.1.call-start = ((), (), s32[]{:S(2)}) async-start(), calls=%async_computation.4 | async-start | bytes 4718592 | tf_op jit(solution)/shard_map/reduce_scatter | solution.py:142
  177.8 194.3 %copy-start.1 = (bf16[64,2,16,256]{3,2,1,0:T(8,128)(2,1)S(1)}, bf16[64,2,16,256]{3,2,1,0:T(8,128)(2,1)}, u32[]{:S(2)}) copy-start(bf16[64,2,16,256]{3,2,1,0:T(8,128)(2,1)} %param.21) | copy-start | bytes 3145732
Sparse Core Ops, SparseCore 0:
  12.0 122.9 all-gather.1
Sparse Core Ops, SparseCore 1:
  59.9 80.2 reduce-scatter.4
  182.6 189.5 reduce-scatter.2
